TPU v7x, 128 devices: a whole 4x4x4 slice. The times are simulated.
128 devices in a mesh: dp: 4 (over x), seq: 8 (over z, core), expert: 4 (over y).
Axes of the slice: x: 4, y: 4, z: 4, core: 2. Of those that a mesh axis runs over, the one named last changes fastest.
Arguments:
- x_in: bfloat16 [4096, 8192], P(('dp', 'seq'), 'expert'), parts along dimension 0, may hold values from -6 to 6
- z_in: bfloat16 [4096, 8192], P(('dp', 'seq'), 'expert'), parts along dimension 0, may hold values from -6 to 6
- step_raw: bfloat16 [4096, 8192], P(('dp', 'seq'), 'expert'), parts along dimension 0, may hold values from -4 to 4
- step_bias: float32 [8192], P('expert'), may hold values from -9 to -2
- decay_rate: float32 [16, 8192], P(None, 'expert'), may hold values from 0.5 to 4
- b_coef: bfloat16 [16, 4096], P(None, ('dp', 'seq')), parts along dimension 1, may hold values from -6 to 6
- c_coef: bfloat16 [16, 4096], P(None, ('dp', 'seq')), parts along dimension 1, may hold values from -6 to 6
- skip_gain: float32 [8192], P('expert'), may hold values from 0.5 to 1.5
- out_proj: bfloat16 [8192, 8192], P('expert', 'seq'), may hold values from -0.0625 to 0.0625
- residual: bfloat16 [4096, 8192], P(('dp', 'seq', 'expert')), parts along dimension 0, may hold values from -6 to 6
- norm_gain: float32 [8192], replicated, may hold values from 0.5 to 1.5
- router_weight: bfloat16 [8192, 16], replicated, may hold values from -0.0625 to 0.0625
- expert_ids: int32 [4096, 2], P(('dp', 'seq', 'expert')), parts along dimension 0, may hold values from 0 to 15, as said below
- gate_weight: bfloat16 [8192, 12288], P(None, ('seq', 'expert')), may hold values from -0.0625 to 0.0625
- up_weight: bfloat16 [8192, 12288], P(None, ('seq', 'expert')), may hold values from -0.0625 to 0.0625
- down_weight: bfloat16 [12288, 8192], P(('seq', 'expert')), may hold values from -0.0546875 to 0.0546875
Outputs:
- final: bfloat16 [4096, 8192], P(('dp', 'seq', 'expert')), parts along dimension 0
There are 4 independent parts, one for each index of `dp`. A program takes and returns all parts, laid end to end along the dimension named above; an argument that names none is the same for every part. Nothing has to cross between parts.
Inputs may be any that keep to these rules, and one draw needn't show every extreme that they name: `expert_ids`: each token names 2 different experts; among the 32 rows of one device at most 16 name expert 0 and at least one does; on some device exactly 16 do.
All inputs are finite; a program needn't handle non-finite values.
Results may differ from a plain program's by a relative error of at most 0.006.
Values may be sent and summed in bfloat16 or wider, within the bound.
No kernel may reach another device: no remote copies, remote signals or barrier semaphores. Data moves between devices by JAX's collectives and lax.ppermute only.
A program may use at most 192 MiB of HBM per device.

v0:
```python
import jax
import jax.numpy as jnp
from jax import lax
from jax.sharding import PartitionSpec as P

BLOCK = 128


def entering(value, axis, join, neutral):
    count, mine = (lax.axis_size(axis), lax.axis_index(axis))
    pieces = jax.tree.map(lambda part: lax.all_gather(part, axis), value)
    running = jax.tree.map(
        lambda part, zero: jnp.full_like(part, 0) + jnp.asarray(zero, part.dtype), value, neutral
    )

    def hop(position, running):
        longer = join(running, jax.tree.map(lambda part: part[position], pieces))
        return jax.tree.map(lambda new, old: jnp.where(position < mine, new, old), longer, running)

    return lax.fori_loop(0, count - 1, hop, running)


def pair_combine(early, later):
    return (early[0] * later[0], later[0] * early[1] + later[1])


def end_state(step_size, x_float, decay_rate, b_rows):

    def end_advance(state, inputs):
        step_now, x_now, b_now = inputs
        state = (
            jnp.exp(-step_now[None, :] * decay_rate) * state
            + (step_now * x_now)[None, :] * b_now[:, None]
        )
        return (state, None)

    start_state = jnp.zeros(decay_rate.shape, jnp.float32)
    final_state, _ = lax.scan(end_advance, start_state, (step_size, x_float, b_rows), unroll=8)
    return final_state


def scan_outputs(state_in, step_size, x_float, decay_rate, b_rows, c_rows, skip_gain):

    def scan_advance(state, inputs):
        step_now, x_now, b_now, c_now = inputs
        state = (
            jnp.exp(-step_now[None, :] * decay_rate) * state
            + (step_now * x_now)[None, :] * b_now[:, None]
        )
        y_now = jnp.sum(c_now[:, None] * state, axis=0) + skip_gain * x_now
        return (state, y_now)

    _, outputs = lax.scan(scan_advance, state_in, (step_size, x_float, b_rows, c_rows), unroll=8)
    return outputs


def on_device(
    x_in,
    z_in,
    step_raw,
    step_bias,
    decay_rate,
    b_coef,
    c_coef,
    skip_gain,
    out_proj,
    residual,
    norm_gain,
    router_weight,
    expert_ids,
    gate_weight,
    up_weight,
    down_weight,
):
    step_size = jax.nn.softplus(step_raw.astype(jnp.float32) + step_bias[None, :])
    x_float = x_in.astype(jnp.float32)
    b_rows = b_coef.astype(jnp.float32).T
    c_rows = c_coef.astype(jnp.float32).T
    state_end = end_state(step_size, x_float, decay_rate, b_rows)
    decay_end = jnp.exp(-decay_rate * jnp.sum(step_size, axis=0)[None, :])
    identity = (jnp.ones_like(decay_end), jnp.zeros_like(state_end))
    carried = entering((decay_end, state_end), "seq", pair_combine, identity)
    state_in = carried[1]
    scanned = scan_outputs(state_in, step_size, x_float, decay_rate, b_rows, c_rows, skip_gain)
    gated = (scanned * jax.nn.silu(z_in.astype(jnp.float32))).astype(jnp.bfloat16)
    column_part = jnp.dot(
        lax.all_gather(gated, "seq", axis=0, tiled=True),
        out_proj,
        preferred_element_type=jnp.float32,
    )
    seq_count = lax.axis_size("seq")
    expert_count = lax.axis_size("expert")
    rows = residual.shape[0]
    grouped = column_part.reshape(seq_count, expert_count, rows, column_part.shape[1])
    summed = lax.psum_scatter(grouped, "expert", scatter_dimension=1, tiled=True)
    arranged = jnp.transpose(summed[:, 0], (1, 0, 2))
    swapped = lax.all_to_all(arranged, "seq", split_axis=1, concat_axis=1, tiled=True)
    mamba_out = swapped.reshape(rows, -1)
    hidden = (residual.astype(jnp.float32) + mamba_out).astype(jnp.bfloat16)
    hidden_f = hidden.astype(jnp.float32)
    width_d = hidden.shape[1]
    scale_cols = width_d // BLOCK
    normed = (
        hidden_f
        * lax.rsqrt(jnp.mean(hidden_f * hidden_f, axis=-1, keepdims=True) + 1e-05)
        * norm_gain[None, :]
    )
    blocked = normed.reshape(rows, scale_cols, BLOCK)
    scales = (jnp.max(jnp.abs(blocked), axis=-1) / 448.0 + 1e-06).astype(jnp.bfloat16)
    quant = (blocked / scales.astype(jnp.float32)[..., None]).astype(jnp.bfloat16)
    restored = (
        (quant.astype(jnp.float32) * scales.astype(jnp.float32)[..., None])
        .astype(jnp.bfloat16)
        .reshape(rows, width_d)
    )
    experts = router_weight.shape[1]
    probs = jax.nn.sigmoid(jnp.dot(restored, router_weight, preferred_element_type=jnp.float32))
    picks = expert_ids[:, :, None] == jnp.arange(experts, dtype=jnp.int32)[None, None, :]
    chosen = jnp.sum(jnp.where(picks, probs[:, None, :], jnp.float32(0.0)), axis=-1)
    weights = chosen / jnp.sum(chosen, axis=-1, keepdims=True)
    coef = jnp.sum(jnp.where(expert_ids == 0, weights, jnp.float32(0.0)), axis=1)
    wanted = jnp.any(expert_ids == 0, axis=1)
    wanted_int = wanted.astype(jnp.int32)
    slot_pos = jnp.cumsum(wanted_int) - wanted_int
    capacity = rows // 2
    table = (
        (slot_pos[None, :] == jnp.arange(capacity, dtype=jnp.int32)[:, None]) & wanted[None, :]
    ).astype(jnp.bfloat16)
    send_quant = jnp.dot(
        table, quant.reshape(rows, width_d), preferred_element_type=jnp.float32
    ).astype(jnp.bfloat16)
    send_scale = jnp.dot(table, scales, preferred_element_type=jnp.float32).astype(jnp.bfloat16)
    all_quant, all_scale = (
        lax.all_gather(send_quant, ("seq", "expert"), axis=0, tiled=True),
        lax.all_gather(send_scale, ("seq", "expert"), axis=0, tiled=True),
    )
    slots = all_quant.shape[0]
    inputs = (
        (
            all_quant.reshape(slots, scale_cols, BLOCK).astype(jnp.float32)
            * all_scale.astype(jnp.float32)[..., None]
        )
        .astype(jnp.bfloat16)
        .reshape(slots, width_d)
    )
    gate_value = jnp.dot(inputs, gate_weight, preferred_element_type=jnp.float32)
    up_value = jnp.dot(inputs, up_weight, preferred_element_type=jnp.float32)
    active = (jax.nn.silu(gate_value) * up_value).astype(jnp.bfloat16)
    own_sum = lax.psum_scatter(
        jnp.dot(active, down_weight, preferred_element_type=jnp.float32).astype(jnp.bfloat16),
        ("seq", "expert"),
        scatter_dimension=0,
        tiled=True,
    )
    returned = jnp.dot(table.T, own_sum, preferred_element_type=jnp.float32)
    return (hidden_f + coef[:, None] * returned).astype(jnp.bfloat16)


def solution(mesh):
    return jax.shard_map(
        on_device,
        mesh=mesh,
        in_specs=(
            P(("dp", "seq"), "expert"),
            P(("dp", "seq"), "expert"),
            P(("dp", "seq"), "expert"),
            P("expert"),
            P(None, "expert"),
            P(None, ("dp", "seq")),
            P(None, ("dp", "seq")),
            P("expert"),
            P("expert", "seq"),
            P(("dp", "seq", "expert"), None),
            P(),
            P(),
            P(("dp", "seq", "expert"), None),
            P(None, ("seq", "expert")),
            P(None, ("seq", "expert")),
            P(("seq", "expert"), None),
        ),
        out_specs=P(("dp", "seq", "expert"), None),
        check_vma=False,
    )
```

profile of v0, /device:TPU:0, one launch (start us, length us, event | category | flops | bytes accessed | tf_op | source)
XLA Modules:
  0.0 533.8 jit_solution(4677953557653513335)
XLA Ops:
  8.5 1.7 fusion.67
  10.2 21.8 %while.38 = (s32[]{:T(128)}, f32[16,2048]{1,0:T(8,128)S(1)}, f32[16,8,2048]{2,1,0:T(8,128)S(1)}, f32[16,2048]{1,0:T(8,128)}, f32[16,8,2048]{2,1,0:T(8,128)S(1)},...) while((s32[]{:T(128)}, f32[16,2048]{1,0:T(8,128)S(1)}, ...), condition=%wide.region_2.3_spmd.clone, body=%wide.region_1.2_spmd.clone.sunk | while | flops 1114122 | bytes 789271 | solution.py:38
  32.8 1.6 multiply_exponential_fusion
  34.6 24.2 %all-gather.13.cloned.1.call-done = f32[128,2048]{1,0:T(8,128)} async-done(((f32[16,2048]{1,0:T(8,128)}), f32[128,2048]{1,0:T(8,128)}) %all-gather.13.cloned.1.call-update) | async-done | bytes 1048592 | tf_op jit(solution)/shard_map/all_gather | solution.py:11
  58.8 25.1 %all-gather.11.cloned.1.call-done = f32[128,2048]{1,0:T(8,128)} async-done(((f32[16,2048]{1,0:T(8,128)}), f32[128,2048]{1,0:T(8,128)}) %all-gather.11.cloned.1.call-update) | async-done | bytes 1048592 | tf_op jit(solution)/shard_map/all_gather | solution.py:11
  84.0 7.6 %while.39 = (s32[]{:T(128)}, f32[16,2048]{1,0:T(8,128)S(1)}, s32[]{:T(128)}, f32[8,16,2048]{2,1,0:T(8,128)}, f32[8,16,2048]{2,1,0:T(8,128)}, /*index=5*/s32[]{:T(128)}, s32[]{:T(128)}) while((s32[]{:T(128)}, f32[16,2048]{1,0:T(8,128)S(1)}, s32[]{:T(128)}, f32[8,16,2048]{2,1,0:T(8,128)}, f32[8,16,2048]{2,1,0:T(8,128)}, ...), condition=%wide.region_4.5_spmd.clone, body=%wide.region_3.4_spmd.clone.sunk | while | flops 131076 | bytes 524397 | solution.py:20
  91.6 71.2 %while.37 = (s32[]{:T(128)}, f32[16,2048]{1,0:T(8,128)S(1)}, f32[16,8,2048]{2,1,0:T(8,128)}, f32[16,8,2048]{2,1,0:T(8,128)S(1)}, f32[16,2048]{1,0:T(8,128)}, /*i...) while((s32[]{:T(128)}, f32[16,2048]{1,0:T(8,128)S(1)}, ...), condition=%wide.region_14.15_spmd, body=%wide.region_5.14_spmd.sunk | while | flops 2408457 | bytes 2078409 | solution.py:53
  97.3 1.2 multiply_reduce_fusion.11
  106.2 1.2 multiply_reduce_fusion.11
  110.7 1.2 multiply_reduce_fusion.11
  162.8 2.3 fusion.66
  165.2 32.3 %all-gather.7.cloned.1.call-done = bf16[1024,2048]{1,0:T(8,128)(2,1)} async-done(((bf16[128,2048]{1,0:T(8,128)(2,1)}), bf16[1024,2048]{1,0:T(8,128)(2,1)}) %all-gather.7.cloned.1.call-update) | async-done | bytes 4194320 | tf_op jit(solution)/shard_map/all_gather | solution.py:87
  197.5 9.9 %fusion.91 = f32[1024,1024]{1,0:T(8,128)} fusion(bf16[1024,2048]{1,0:T(8,128)(2,1)} %all-gather.7.cloned.1.call-done, bf16[2048,1024]{1,0:T(8,128)(2,1)} %param.30), kind=kOutput, calls=%fused_computation.200 | convolution fusion | flops 4294967296 | bytes 12582912 | tf_op jit(solution)/shard_map/dot_general | solution.py:86
  208.0 92.1 %all-reduce.3.cloned.1.call-done = f32[8,4,32,1024]{3,2,1,0:T(8,128)} async-done(((f32[8,4,32,1024]{3,2,1,0:T(8,128)}), f32[8,4,32,1024]{3,2,1,0:T(8,128)}) %all-reduce.3.cloned.1.call-update) | async-done | bytes 4194320
  300.2 3.0 dynamic-slice_bitcast_fusion
  303.1 4.4 all-to-all-start
  307.9 15.6 %all-to-all-done = f32[32,8,1024]{2,0,1:T(8,128)S(1)} async-done(((f32[32,8,1024]{2,0,1:T(8,128)}), f32[32,8,1024]{2,0,1:T(8,128)S(1)}, u32[]{:S(2)}, u32[]{:S(2)}) %all-to-all-start) | async-done | bytes 1048608 | tf_op jit(solution)/shard_map/all_to_all | solution.py:97
  326.7 38.1 %all_gather.27 = bf16[512,64]{1,0:T(8,128)(2,1)S(1)} all-gather(bf16[16,64]{1,0:T(8,128)(2,1)S(1)} %convolution_convert_fusion.2), channel_id=1, replica_groups=mesh['dp'=4,'seq'=8,'expert'=4] {'seq','expert'}, dimensions={0}, use_global_device_ids=true | all-gather | bytes 67584 | tf_op jit(solution)/shard_map/all_gather | solution.py:135
  364.9 12.8 %all-gather.9.cloned.1.call-done = bf16[512,8192]{1,0:T(8,128)(2,1)} async-done(((bf16[16,8192]{1,0:T(8,128)(2,1)}), bf16[512,8192]{1,0:T(8,128)(2,1)}) %all-gather.9.cloned.1.call-update) | async-done | bytes 8388624 | tf_op jit(solution)/shard_map/all_gather | solution.py:134
  377.7 8.0 %mul.821 = f32[512,64,128]{2,1,0:T(8,128)} broadcast(bf16[512,64]{1,0:T(8,128)(2,1)S(1)} %all_gather.27), dimensions={0,1} | broadcast | bytes 16842752 | tf_op jit(solution)/shard_map/mul | solution.py:140
  385.6 18.4 %fusion.89 = f32[512,384]{1,0:T(8,128)S(1)} fusion(bf16[8192,384]{1,0:T(8,128)(2,1)} %param.35, f32[64,8,64,128]{3,2,1,0:T(8,128)} %bitcast.286, bf16[512,8192]{1,0:T(8,128)(2,1)S(1)} %copy-done.1), kind=kOutput, calls=%fused_computation.199 | convolution fusion | flops 3233808384 | bytes 32243712 | tf_op jit(solution)/shard_map/dot_general | solution.py:146
  404.0 28.3 %convolution_convert_fusion = bf16[512,8192]{1,0:T(8,128)(2,1)} fusion(bf16[384,8192]{1,0:T(8,128)(2,1)} %param.37, bf16[8192,384]{1,0:T(8,128)(2,1)} %param.36, f32[512,384]{1,0:T(8,128)S(1)} %fusion.89, f32[64,8,64,128]{3,2,1,0:T(8,128)} %bitcast.287, bf16[512,8192]{1,0:T(8,128)(2,1)} %all-gather.9.cloned.1.call-done), kind=kOutput, calls=%fused_computation.137 | convolution fusion | flops 6460407808 | bytes 46923776 | tf_op jit(solution)/shard_map/dot_general | solution.py:150
  433.2 91.7 %reduce-scatter.5.cloned.1.call-done = bf16[16,8192]{1,0:T(8,128)(2,1)} async-done(((bf16[512,8192]{1,0:T(8,128)(2,1)}), bf16[16,8192]{1,0:T(8,128)(2,1)}) %reduce-scatter.5.cloned.1.call-update) | async-done | bytes 262160 | tf_op jit(solution)/shard_map/reduce_scatter | solution.py:149
  524.9 2.1 fusion.50
  (289 shorter events, 103.5 us)
Async XLA Ops:
  6.5 425.8 %copy-start = (bf16[8192,16]{0,1:T(8,128)(2,1)S(1)}, bf16[8192,16]{0,1:T(8,128)(2,1)}, u32[]{:S(2)}) copy-start(bf16[8192,16]{0,1:T(8,128)(2,1)} %param.33) | copy-start | bytes 786436
  6.5 27.9 %copy-start.7 = (bf16[16,128]{1,0:T(8,128)(2,1)S(1)}, bf16[16,128]{1,0:T(8,128)(2,1)}, u32[]{:S(2)}) copy-start(bf16[16,128]{1,0:T(8,128)(2,1)} %param.28) | copy-start | bytes 12292
  6.5 85.0 %copy-start.5 = (f32[2048]{0:T(1024)S(1)}, f32[2048]{0:T(1024)}, u32[]{:S(2)}) copy-start(f32[2048]{0:T(1024)} %param.29) | copy-start | bytes 24580
  6.5 52.3 %all-gather.13.cloned.1.call-start = ((), (), s32[]{:S(2)}) async-start(), calls=%async_computation.6 | async-start | bytes 1179648 | tf_op jit(solution)/shard_map/all_gather | solution.py:11
  32.1 0.6 copy-start.2
  32.1 130.7 %copy-start.4 = (bf16[128,2048]{1,0:T(8,128)(2,1)S(1)}, bf16[128,2048]{1,0:T(8,128)(2,1)}, u32[]{:S(2)}) copy-start(bf16[128,2048]{1,0:T(8,128)(2,1)} %param.23) | copy-start | bytes 1572868
  32.7 51.2 %all-gather.11.cloned.1.call-start = ((), (), s32[]{:S(2)}) async-start(), calls=%async_computation.5 | async-start | bytes 1179648 | tf_op jit(solution)/shard_map/all_gather | solution.py:11
  34.4 163.1 %all-gather.7.cloned.1.call-start = ((), (), s32[]{:S(2)}) async-start(), calls=%async_computation.2 | async-start | bytes 4718592 | tf_op jit(solution)/shard_map/all_gather | solution.py:87
  165.1 42.3 %copy-start.9 = (u32[128]{0:T(128)S(1)}, u32[128]{0:T(128)}, u32[]{:S(2)}) copy-start(u32[128]{0:T(128)} %constant.87) | copy-start | bytes 1540
  165.2 135.0 %all-reduce.3.cloned.1.call-start = ((), (), s32[]{:S(2)}) async-start(), calls=%async_computation.7 | async-start | bytes 8388608
  207.4 100.2 %copy-start.8 = (s32[32,2]{0,1:T(2,128)S(1)}, s32[32,2]{0,1:T(2,128)}, u32[]{:S(2)}) copy-start(s32[32,2]{0,1:T(2,128)} %param.34) | copy-start | bytes 772
  207.4 116.2 %copy-start.3 = (bf16[32,8192]{1,0:T(8,128)(2,1)S(1)}, bf16[32,8192]{1,0:T(8,128)(2,1)}, u32[]{:S(2)}) copy-start(bf16[32,8192]{1,0:T(8,128)(2,1)} %param.31) | copy-start | bytes 1572868
  207.4 116.5 %copy-start.6 = (f32[8192]{0:T(1024)S(1)}, f32[8192]{0:T(1024)}, u32[]{:S(2)}) copy-start(f32[8192]{0:T(1024)} %param.32) | copy-start | bytes 98308
  303.1 20.4 %all-to-all-start = ((f32[32,8,1024]{2,0,1:T(8,128)}), f32[32,8,1024]{2,0,1:T(8,128)S(1)}, u32[]{:S(2)}, u32[]{:S(2)}) async-start(f32[32,8,1024]{2,0,1:T(8,128)} %dynamic-slice_bitcast_fusion), calls=%async_computation | async-start | bytes 2097152 | tf_op jit(solution)/shard_map/all_to_all | solution.py:97
  307.5 70.1 %all-gather.9.cloned.1.call-start = ((), (), s32[]{:S(2)}) async-start(), calls=%async_computation.3 | async-start | bytes 8650752 | tf_op jit(solution)/shard_map/all_gather | solution.py:134
  326.6 198.3 %reduce-scatter.5.cloned.1.call-start = ((), (), s32[]{:S(2)}) async-start(), calls=%async_computation.4 | async-start | bytes 8650752 | tf_op jit(solution)/shard_map/reduce_scatter | solution.py:149
  377.7 8.0 %copy-start.1 = (bf16[512,8192]{1,0:T(8,128)(2,1)S(1)}, bf16[512,8192]{1,0:T(8,128)(2,1)}, u32[]{:S(2)}) copy-start(bf16[512,8192]{1,0:T(8,128)(2,1)} %all-gather.9.cloned.1.call-done) | copy-start | bytes 25165828
Sparse Core Ops, SparseCore 0:
  32.9 25.9 all-gather.12
  60.5 23.3 all-gather.10
  165.3 32.1 all-gather.6
  207.6 92.5 all-reduce.2
  326.7 50.9 all-gather.8
  432.5 92.3 reduce-scatter.4
where the time goes:
time: 535 us; the launch traced here: 534 us
  waiting for transfers between devices  294 us (55%)
  other arithmetic  96.1 us (18%)
  matrix products  60.5 us (11%)
  blocking collectives  38.1 us (7%)
  local copies, waits for them, and re-layouts  25.5 us (5%)
  between operations  13.7 us (3%)
    unnamed x7, waiting for transfers between devices  92.2 us
    reduce_scatter x1, waiting for transfers between devices, on_device(): lax.psum_scatter(jnp.dot(active, down_weight, preferred_element_type=jnp....  91.7 us
    reduce_sum x48, other arithmetic, scan_advance(): y_now = jnp.sum(c_now[:, None] * state, axis=0) + skip_gain * x_now  54.8 us
    all_gather x2, waiting for transfers between devices, entering(): pieces = jax.tree.map(lambda part: lax.all_gather(part, axis), value)  49.4 us
    all_gather x1, blocking collectives, on_device(): lax.all_gather(send_scale, ('seq', 'expert'), axis=0, tiled=True)  38.1 us
    all_gather x1, waiting for transfers between devices, on_device(): lax.all_gather(gated, 'seq', axis=0, tiled=True)  32.3 us
    dot_general x1, matrix products, on_device(): jnp.dot(active, down_weight, preferred_element_type=jnp.float32)  28.3 us
    add x16, other arithmetic, end_advance(): jnp.exp(-step_now[None, :] * decay_rate) * state  18.7 us
  transfers between devices with their start and end apart: 7, of which 7 were waited for; matrix products, arithmetic and copies ran while one was open for 1% of the time, Pallas kernels for 0%

commit v1 on v0

--- a/solution.py
+++ b/solution.py
@@ -2,6 +2,7 @@
 import jax.numpy as jnp
 from jax import lax
 from jax.sharding import PartitionSpec as P
+from jax.lax import all_to_all, axis_size
 
 BLOCK = 128
 
@@ -84,7 +85,10 @@
     scanned = scan_outputs(state_in, step_size, x_float, decay_rate, b_rows, c_rows, skip_gain)
     gated = (scanned * jax.nn.silu(z_in.astype(jnp.float32))).astype(jnp.bfloat16)
     column_part = jnp.dot(
-        lax.all_gather(gated, "seq", axis=0, tiled=True),
+        jnp.concatenate(
+            all_to_all(jnp.stack([gated for _ in range(axis_size("seq"))], axis=0), "seq", 0, 0),
+            axis=0,
+        ),
         out_proj,
         preferred_element_type=jnp.float32,
     )

time: 535 us -> 551 us (1.030)
  blocking collectives: 38.1 us -> 90.8 us
  waiting for transfers between devices: 294 us -> 261 us
    all_to_all x0 -> x1, blocking collectives: none -> 52.7 us  [on_device(): all_to_all(jnp.stack([gated for _ in range(axis_size('seq'))], axis=0), '...]
    all_gather x1 -> x0, waiting for transfers between devices: 32.3 us -> none  [on_device(): lax.all_gather(gated, 'seq', axis=0, tiled=True)]
    unnamed x7 -> x6, waiting for transfers between devices: 92.2 us -> 91.7 us
  transfers between devices with their start and end apart: 7 -> 6, of which waited for: 7 -> 6; matrix products, arithmetic and copies ran while one was open for 1% -> 1% of each run, Pallas kernels for 0% -> 0%
where the time goes in v1:
time: 551 us; the launch traced here: 549 us
  waiting for transfers between devices  261 us (47%)
  other arithmetic  95.3 us (17%)
  blocking collectives  90.8 us (16%)
  matrix products  56.6 us (10%)
  local copies, waits for them, and re-layouts  26 us (5%)
  between operations  13.4 us (2%)
    reduce_scatter x1, waiting for transfers between devices, on_device(): lax.psum_scatter(jnp.dot(active, down_weight, preferred_element_type=jnp....  91.7 us
    unnamed x6, waiting for transfers between devices  91.7 us
    reduce_sum x48, other arithmetic, scan_advance(): y_now = jnp.sum(c_now[:, None] * state, axis=0) + skip_gain * x_now  54.8 us
    all_to_all x1, blocking collectives, on_device(): all_to_all(jnp.stack([gated for _ in range(axis_size('seq'))], axis=0), '...  52.7 us
    all_gather x2, waiting for transfers between devices, entering(): pieces = jax.tree.map(lambda part: lax.all_gather(part, axis), value)  49.4 us
    all_gather x1, blocking collectives, on_device(): lax.all_gather(send_scale, ('seq', 'expert'), axis=0, tiled=True)  38.1 us
    dot_general x1, matrix products, on_device(): jnp.dot(active, down_weight, preferred_element_type=jnp.float32)  28.3 us
    add x16, other arithmetic, end_advance(): jnp.exp(-step_now[None, :] * decay_rate) * state  18.7 us
  transfers between devices with their start and end apart: 6, of which 6 were waited for; matrix products, arithmetic and copies ran while one was open for 1% of the time, Pallas kernels for 0%

profile of v1, /device:TPU:0, one launch (start us, length us, event | category | flops | bytes accessed | tf_op | source)
XLA Modules:
  0.0 549.2 jit_solution(2201608740314228060)
XLA Ops:
  8.5 1.7 fusion.69
  10.2 21.8 %while.38 = (s32[]{:T(128)}, f32[16,2048]{1,0:T(8,128)S(1)}, f32[16,8,2048]{2,1,0:T(8,128)S(1)}, f32[16,2048]{1,0:T(8,128)}, f32[16,8,2048]{2,1,0:T(8,128)S(1)},...) while((s32[]{:T(128)}, f32[16,2048]{1,0:T(8,128)S(1)}, ...), condition=%wide.region_2.3_spmd.clone, body=%wide.region_1.2_spmd.clone.sunk | while | flops 1114122 | bytes 789271 | solution.py:39
  32.8 1.6 multiply_exponential_fusion
  34.6 24.2 %all-gather.10.cloned.1.call-done = f32[128,2048]{1,0:T(8,128)} async-done(((f32[16,2048]{1,0:T(8,128)}), f32[128,2048]{1,0:T(8,128)}) %all-gather.10.cloned.1.call-update) | async-done | bytes 1048592 | tf_op jit(solution)/shard_map/all_gather | solution.py:12
  58.8 25.1 %all-gather.8.cloned.1.call-done = f32[128,2048]{1,0:T(8,128)} async-done(((f32[16,2048]{1,0:T(8,128)}), f32[128,2048]{1,0:T(8,128)}) %all-gather.8.cloned.1.call-update) | async-done | bytes 1048592 | tf_op jit(solution)/shard_map/all_gather | solution.py:12
  84.0 7.6 %while.39 = (s32[]{:T(128)}, f32[16,2048]{1,0:T(8,128)S(1)}, s32[]{:T(128)}, f32[8,16,2048]{2,1,0:T(8,128)}, f32[8,16,2048]{2,1,0:T(8,128)}, /*index=5*/s32[]{:T(128)}, s32[]{:T(128)}) while((s32[]{:T(128)}, f32[16,2048]{1,0:T(8,128)S(1)}, s32[]{:T(128)}, f32[8,16,2048]{2,1,0:T(8,128)}, f32[8,16,2048]{2,1,0:T(8,128)}, ...), condition=%wide.region_4.5_spmd.clone, body=%wide.region_3.4_spmd.clone.sunk | while | flops 131076 | bytes 524397 | solution.py:21
  91.6 71.2 %while.37 = (s32[]{:T(128)}, f32[16,2048]{1,0:T(8,128)S(1)}, f32[16,8,2048]{2,1,0:T(8,128)}, f32[16,8,2048]{2,1,0:T(8,128)S(1)}, f32[16,2048]{1,0:T(8,128)}, /*i...) while((s32[]{:T(128)}, f32[16,2048]{1,0:T(8,128)S(1)}, ...), condition=%wide.region_14.15_spmd, body=%wide.region_5.14_spmd.sunk | while | flops 2408457 | bytes 2078409 | solution.py:54
  92.9 1.2 multiply_reduce_fusion.11
  101.8 1.2 multiply_reduce_fusion.11
  115.1 1.2 multiply_reduce_fusion.11
  162.8 1.5 fusion.68
  164.9 52.7 %all_to_all.10 = bf16[8,128,2048]{2,1,0:T(8,128)(2,1)S(1)} all-to-all(bf16[8,128,2048]{2,1,0:T(8,128)(2,1)S(1)} %stack.2), channel_id=1, replica_groups=mesh['dp'=4,'seq'=8,'expert'=4] {'seq'}, dimensions={0} | all-to-all | bytes 8388608 | tf_op jit(solution)/shard_map/all_to_all | solution.py:89
  217.6 6.0 %fusion.51 = f32[8,4,32,1024]{3,2,1,0:T(8,128)} fusion(bf16[8,4,32,2048]{3,2,1,0:T(8,128)(2,1)S(1)} %bitcast.295, bf16[2048,1024]{1,0:T(8,128)(2,1)S(1)} %copy-done.9), kind=kOutput, calls=%fused_computation.142 | convolution fusion | flops 4294967296 | bytes 12582912 | tf_op jit(solution)/shard_map/dot_general | solution.py:87
  224.2 91.6 %all-reduce.3.cloned.1.call-done = f32[8,4,32,1024]{3,2,1,0:T(8,128)} async-done(((f32[8,4,32,1024]{3,2,1,0:T(8,128)}), f32[8,4,32,1024]{3,2,1,0:T(8,128)}) %all-reduce.3.cloned.1.call-update) | async-done | bytes 4194320
  315.9 3.0 dynamic-slice_bitcast_fusion
  318.8 4.4 all-to-all-start.1
  323.6 15.6 %all-to-all-done.1 = f32[32,8,1024]{2,0,1:T(8,128)S(1)} async-done(((f32[32,8,1024]{2,0,1:T(8,128)}), f32[32,8,1024]{2,0,1:T(8,128)S(1)}, u32[]{:S(2)}, u32[]{:S(2)}) %all-to-all-start.1) | async-done | bytes 1048608 | tf_op jit(solution)/shard_map/all_to_all | solution.py:101
  342.4 38.1 %all_gather.23 = bf16[512,64]{1,0:T(8,128)(2,1)S(1)} all-gather(bf16[16,64]{1,0:T(8,128)(2,1)S(1)} %convolution_convert_fusion.2), channel_id=1, replica_groups=mesh['dp'=4,'seq'=8,'expert'=4] {'seq','expert'}, dimensions={0}, use_global_device_ids=true | all-gather | bytes 67584 | tf_op jit(solution)/shard_map/all_gather | solution.py:139
  380.6 12.8 %all-gather.6.cloned.1.call-done = bf16[512,8192]{1,0:T(8,128)(2,1)} async-done(((bf16[16,8192]{1,0:T(8,128)(2,1)}), bf16[512,8192]{1,0:T(8,128)(2,1)}) %all-gather.6.cloned.1.call-update) | async-done | bytes 8388624 | tf_op jit(solution)/shard_map/all_gather | solution.py:138
  393.4 8.0 %mul.821 = f32[512,64,128]{2,1,0:T(8,128)} broadcast(bf16[512,64]{1,0:T(8,128)(2,1)S(1)} %all_gather.23), dimensions={0,1} | broadcast | bytes 16842752 | tf_op jit(solution)/shard_map/mul | solution.py:144
  401.4 18.4 %fusion.91 = f32[512,384]{1,0:T(8,128)S(1)} fusion(bf16[8192,384]{1,0:T(8,128)(2,1)} %param.35, f32[64,8,64,128]{3,2,1,0:T(8,128)} %bitcast.290, bf16[512,8192]{1,0:T(8,128)(2,1)S(1)} %copy-done.1), kind=kOutput, calls=%fused_computation.201 | convolution fusion | flops 3233808384 | bytes 32243712 | tf_op jit(solution)/shard_map/dot_general | solution.py:150
  419.7 28.3 %convolution_convert_fusion = bf16[512,8192]{1,0:T(8,128)(2,1)} fusion(bf16[384,8192]{1,0:T(8,128)(2,1)} %param.37, bf16[8192,384]{1,0:T(8,128)(2,1)} %param.36, f32[512,384]{1,0:T(8,128)S(1)} %fusion.91, f32[64,8,64,128]{3,2,1,0:T(8,128)} %bitcast.291, bf16[512,8192]{1,0:T(8,128)(2,1)} %all-gather.6.cloned.1.call-done), kind=kOutput, calls=%fused_computation.137 | convolution fusion | flops 6460407808 | bytes 46923776 | tf_op jit(solution)/shard_map/dot_general | solution.py:154
  448.9 91.7 %reduce-scatter.5.cloned.1.call-done = bf16[16,8192]{1,0:T(8,128)(2,1)} async-done(((bf16[512,8192]{1,0:T(8,128)(2,1)}), bf16[16,8192]{1,0:T(8,128)(2,1)}) %reduce-scatter.5.cloned.1.call-update) | async-done | bytes 262160 | tf_op jit(solution)/shard_map/reduce_scatter | solution.py:153
  540.6 2.1 fusion.50
  (290 shorter events, 104.0 us)
Async XLA Ops:
  6.5 441.5 %copy-start = (bf16[8192,16]{0,1:T(8,128)(2,1)S(1)}, bf16[8192,16]{0,1:T(8,128)(2,1)}, u32[]{:S(2)}) copy-start(bf16[8192,16]{0,1:T(8,128)(2,1)} %param.33) | copy-start | bytes 786436
  6.5 27.9 %copy-start.7 = (bf16[16,128]{1,0:T(8,128)(2,1)S(1)}, bf16[16,128]{1,0:T(8,128)(2,1)}, u32[]{:S(2)}) copy-start(bf16[16,128]{1,0:T(8,128)(2,1)} %param.28) | copy-start | bytes 12292
  6.5 85.1 %copy-start.5 = (f32[2048]{0:T(1024)S(1)}, f32[2048]{0:T(1024)}, u32[]{:S(2)}) copy-start(f32[2048]{0:T(1024)} %param.29) | copy-start | bytes 24580
  6.5 52.3 %all-gather.10.cloned.1.call-start = ((), (), s32[]{:S(2)}) async-start(), calls=%async_computation.6 | async-start | bytes 1179648 | tf_op jit(solution)/shard_map/all_gather | solution.py:12
  32.1 0.6 copy-start.2
  32.7 51.2 %all-gather.8.cloned.1.call-start = ((), (), s32[]{:S(2)}) async-start(), calls=%async_computation.5 | async-start | bytes 1179648 | tf_op jit(solution)/shard_map/all_gather | solution.py:12
  34.4 281.5 %all-reduce.3.cloned.1.call-start = ((), (), s32[]{:S(2)}) async-start(), calls=%async_computation.7 | async-start | bytes 8388608
  91.6 71.2 %copy-start.4 = (bf16[128,2048]{1,0:T(8,128)(2,1)S(1)}, bf16[128,2048]{1,0:T(8,128)(2,1)}, u32[]{:S(2)}) copy-start(bf16[128,2048]{1,0:T(8,128)(2,1)} %param.23) | copy-start | bytes 1572868
  164.3 53.2 %copy-start.9 = (bf16[2048,1024]{1,0:T(8,128)(2,1)S(1)}, bf16[2048,1024]{1,0:T(8,128)(2,1)}, u32[]{:S(2)}) copy-start(bf16[2048,1024]{1,0:T(8,128)(2,1)} %param.30) | copy-start | bytes 12582916
  217.6 6.1 %copy-start.10 = (u32[128]{0:T(128)S(1)}, u32[128]{0:T(128)}, u32[]{:S(2)}) copy-start(u32[128]{0:T(128)} %constant.87) | copy-start | bytes 1540
  223.6 99.7 %copy-start.8 = (s32[32,2]{0,1:T(2,128)S(1)}, s32[32,2]{0,1:T(2,128)}, u32[]{:S(2)}) copy-start(s32[32,2]{0,1:T(2,128)} %param.34) | copy-start | bytes 772
  223.6 115.7 %copy-start.3 = (bf16[32,8192]{1,0:T(8,128)(2,1)S(1)}, bf16[32,8192]{1,0:T(8,128)(2,1)}, u32[]{:S(2)}) copy-start(bf16[32,8192]{1,0:T(8,128)(2,1)} %param.31) | copy-start | bytes 1572868
  223.6 116.0 %copy-start.6 = (f32[8192]{0:T(1024)S(1)}, f32[8192]{0:T(1024)}, u32[]{:S(2)}) copy-start(f32[8192]{0:T(1024)} %param.32) | copy-start | bytes 98308
  318.8 20.4 %all-to-all-start.1 = ((f32[32,8,1024]{2,0,1:T(8,128)}), f32[32,8,1024]{2,0,1:T(8,128)S(1)}, u32[]{:S(2)}, u32[]{:S(2)}) async-start(f32[32,8,1024]{2,0,1:T(8,128)} %dynamic-slice_bitcast_fusion), calls=%async_computation.1 | async-start | bytes 2097152 | tf_op jit(solution)/shard_map/all_to_all | solution.py:101
  323.2 70.1 %all-gather.6.cloned.1.call-start = ((), (), s32[]{:S(2)}) async-start(), calls=%async_computation.3 | async-start | bytes 8650752 | tf_op jit(solution)/shard_map/all_gather | solution.py:138
  342.3 198.4 %reduce-scatter.5.cloned.1.call-start = ((), (), s32[]{:S(2)}) async-start(), calls=%async_computation.4 | async-start | bytes 8650752 | tf_op jit(solution)/shard_map/reduce_scatter | solution.py:153
  393.4 8.0 %copy-start.1 = (bf16[512,8192]{1,0:T(8,128)(2,1)S(1)}, bf16[512,8192]{1,0:T(8,128)(2,1)}, u32[]{:S(2)}) copy-start(bf16[512,8192]{1,0:T(8,128)(2,1)} %all-gather.6.cloned.1.call-done) | copy-start | bytes 25165828
Sparse Core Ops, SparseCore 0:
  32.9 25.9 all-gather.9
  60.5 23.3 all-gather.7
  223.8 92.0 all-reduce.2
  342.4 50.9 all-gather.5
  448.2 92.3 reduce-scatter.4
